TPU v7x, 32 devices: a whole 2x2x4 slice. The times are simulated.
32 devices in a mesh: fsdp: 8 (over z, y), rows: 4 (over x, core).
Axes of the slice: x: 2, y: 2, z: 4, core: 2. Of those that a mesh axis runs over, the one named last changes fastest.
Arguments:
- frames: bfloat16 [8, 12, 16, 1536], P('fsdp', 'rows'), may hold values from -6 to 6
- kernel: float32 [7, 7, 1536], replicated, may hold values from -0.875 to 0.875
- kernel_bias: float32 [1536], replicated, may hold values from -3 to 3
- layer_norm_weight: float32 [1536], replicated, may hold values from 0.25 to 1.75
- layer_norm_bias: float32 [1536], replicated, may hold values from -3 to 3
- up_weight: bfloat16 [1536, 6144], P('fsdp', 'rows'), may hold values from -1 to 1, as said below
- up_bias: float32 [6144], P('rows'), may hold values from -3 to 3
- grn_gamma: float32 [6144], P('rows'), may hold values from 0.2 to 1
- grn_beta: float32 [6144], P('rows'), may hold values from -3 to 3
- grad_out: bfloat16 [8, 12, 16, 6144], P('fsdp', None, None, 'rows'), may hold values from -8 to 8, as said below
Outputs:
- activation: bfloat16 [8, 12, 16, 6144], P('fsdp', None, None, 'rows')
- frames_grad: bfloat16 [8, 12, 16, 1536], P('fsdp', 'rows')
- up_weight_grad: float32 [1536, 6144], P('fsdp', 'rows')
- kernel_grad: float32 [7, 7, 1536], replicated
Inputs may be any that keep to these rules, and one draw needn't show every extreme that they name: `up_weight`: entries lie within the bounds. `grad_out`: entries lie within the bounds.
All inputs are finite; a program needn't handle non-finite values.
Results may differ from a plain program's by a relative error of at most 0.014.
Values may be sent and summed in bfloat16 or wider, within the bound.
No kernel may reach another device: no remote copies, remote signals or barrier semaphores. Data moves between devices by JAX's collectives and lax.ppermute only.
A program may use at most 64 MiB of HBM per device.

v0:
```python
import jax
import jax.numpy as jnp
from jax import lax
from jax.sharding import PartitionSpec as P

FF = 6144


def extended(block, sides, width):
    for axis, dim in sides:
        count = lax.axis_size(axis)
        forward = [(i, i + 1) for i in range(count - 1)]
        backward = [(target, source) for source, target in forward]
        low = lax.ppermute(
            lax.slice_in_dim(block, block.shape[dim] - width, None, axis=dim), axis, forward
        )
        high = lax.ppermute(lax.slice_in_dim(block, 0, width, axis=dim), axis, backward)
        block = jnp.concatenate([low, block, high], axis=dim)
    return block


def conv_rows(framed, kern, kbias):
    rows = framed.shape[0] - 6
    cols = framed.shape[1]
    wide = jnp.pad(framed, ((0, 0), (3, 3), (0, 0)))
    total = jnp.zeros((rows, cols, framed.shape[2]), jnp.float32) + kbias
    for i in range(kern.shape[0]):
        for j in range(kern.shape[1]):
            total = total + wide[i : i + rows, j : j + cols].astype(jnp.float32) * kern[i, j]
    return total


def back_conv(grad_pad, kern):
    rows = grad_pad.shape[0] - 6
    cols = grad_pad.shape[1]
    wide = jnp.pad(grad_pad, ((0, 0), (3, 3), (0, 0)))
    total = jnp.zeros((rows, cols, grad_pad.shape[2]), jnp.float32)
    for i in range(kern.shape[0]):
        for j in range(kern.shape[1]):
            total = (
                total
                + wide[6 - i : 6 - i + rows, 6 - j : 6 - j + cols].astype(jnp.float32) * kern[i, j]
            )
    return total


def kern_grad(framed, grad_rows):
    rows = grad_rows.shape[0]
    cols = grad_rows.shape[1]
    wide = jnp.pad(framed, ((0, 0), (3, 3), (0, 0)))
    grad_f = grad_rows.astype(jnp.float32)
    parts = []
    for i in range(7):
        for j in range(7):
            parts.append(
                jnp.sum(wide[i : i + rows, j : j + cols].astype(jnp.float32) * grad_f, axis=(0, 1))
            )
    return jnp.stack(parts).reshape(7, 7, grad_rows.shape[2])


def apply_layer_norm(activation_rows, scale_factor, offset_bias):
    centered_input = activation_rows - jnp.mean(activation_rows, axis=-1, keepdims=True)
    inverse_deviation = lax.rsqrt(
        jnp.mean(centered_input * centered_input, axis=-1, keepdims=True) + 1e-06
    )
    standardized_input = centered_input * inverse_deviation
    return (
        (standardized_input * scale_factor + offset_bias).astype(jnp.bfloat16),
        standardized_input,
        inverse_deviation,
    )


def gelu_grad(value):
    return (
        0.5 * (1.0 + jax.scipy.special.erf(value * 0.7071067811865476))
        + value * jnp.exp(-0.5 * value * value) * 0.3989422804014327
    )


def layer_norm_backward(normed_input_gradient, scale_factor, standardized_input, inverse_deviation):
    scaled_output = normed_input_gradient * scale_factor
    return (
        inverse_deviation
        * (
            scaled_output
            - jnp.mean(scaled_output, axis=-1, keepdims=True)
            - standardized_input
            * jnp.mean(scaled_output * standardized_input, axis=-1, keepdims=True)
        )
    ).astype(jnp.bfloat16)


def body(
    frames,
    kernel,
    kernel_bias,
    layer_norm_weight,
    layer_norm_bias,
    up_weight,
    up_bias,
    grn_gamma,
    grn_beta,
    grad_out,
):
    slab = frames[0]
    chans = slab.shape[2]
    columns = lax.all_gather(up_weight, "fsdp", axis=0, tiled=True)
    padded = extended(slab, (("rows", 0),), 3)
    activation_rows = conv_rows(padded, kernel, kernel_bias)
    normed_output, standardized_input, inverse_deviation = apply_layer_norm(
        activation_rows, layer_norm_weight, layer_norm_bias
    )
    whole = lax.all_gather(normed_output, "rows", axis=0, tiled=True)
    height = whole.shape[0]
    cols = whole.shape[1]
    flat = whole.reshape(-1, chans)
    pre = jnp.dot(flat, columns, preferred_element_type=jnp.float32) + up_bias
    post = jax.nn.gelu(pre, approximate=False)
    norms = jnp.sqrt(jnp.sum(post * post, axis=0) + 1e-06)
    cot_f = grad_out[0].reshape(flat.shape[0], -1).astype(jnp.float32)
    dnorm = grn_gamma * jnp.sum(cot_f * post, axis=0)
    norm_total = lax.psum(jnp.sum(norms), "rows")
    denom = norm_total / FF + 1e-06
    ratio = norms / denom
    output = (grn_gamma * (post * ratio) + grn_beta + post).astype(jnp.bfloat16)
    cross = lax.psum(jnp.sum(dnorm * norms), "rows")
    dnorms = dnorm / denom - cross / (denom * denom) / FF
    dpost = cot_f * (1.0 + grn_gamma * ratio) + post * (dnorms / norms)
    dpre = (dpost * gelu_grad(pre)).astype(jnp.bfloat16)
    w_term = lax.dot_general(
        flat, dpre, (((0,), (0,)), ((), ())), preferred_element_type=jnp.float32
    )
    up_grad = lax.psum_scatter(
        w_term.astype(jnp.bfloat16), "fsdp", scatter_dimension=0, tiled=True
    ).astype(jnp.float32)
    dpre_rows = dpre.reshape(height, cols, -1)
    normed_input_gradient = lax.psum_scatter(
        jnp.einsum("hwf,cf->hwc", dpre_rows, columns, preferred_element_type=jnp.float32).astype(
            jnp.bfloat16
        ),
        "rows",
        scatter_dimension=0,
        tiled=True,
    ).astype(jnp.float32)
    activation_gradient = layer_norm_backward(
        normed_input_gradient, layer_norm_weight, standardized_input, inverse_deviation
    )
    grad_pad = extended(activation_gradient, (("rows", 0),), 3)
    dframe = back_conv(grad_pad, kernel).astype(jnp.bfloat16)
    kernel_local = kern_grad(padded, activation_gradient)
    kernel_total = lax.psum(kernel_local, ("fsdp", "rows"))
    activation = output.reshape(1, height, cols, -1)
    return (activation, dframe.reshape((1,) + dframe.shape), up_grad, kernel_total)


def solution(mesh):
    placed = (
        P("fsdp", "rows", None, None),
        P(),
        P(),
        P(),
        P(),
        P("fsdp", "rows"),
        P("rows"),
        P("rows"),
        P("rows"),
        P("fsdp", None, None, "rows"),
    )
    return jax.shard_map(
        body,
        mesh=mesh,
        in_specs=placed,
        out_specs=(
            P("fsdp", None, None, "rows"),
            P("fsdp", "rows", None, None),
            P("fsdp", "rows"),
            P(),
        ),
        check_vma=False,
    )
```

profile of v0, /device:TPU:1, one launch (start us, length us, event | category | flops | bytes accessed | tf_op | source)
XLA Modules:
  0.0 376.6 jit_solution(9324311914852352310)
XLA Ops:
  7.2 0.0 all-gather.2.cloned.1.call-start
  7.2 0.7 all-gather.2.cloned.1.call-update
  7.9 0.0 reduce-scatter.3.cloned.1.call-start
  8.0 2.0 collective-permute-start.1
  9.9 4.5 %collective-permute-start = (bf16[3,16,1536]{2,1,0:T(8,128)(2,1)}, bf16[3,16,1536]{2,1,0:T(8,128)(2,1)S(1)}, u32[]{:S(2)}, u32[]{:S(2)}) collective-permute-start(bf16[3,16,1536]{2,1,0:T(8,128)(2,1)} %bitcast.25), channel_id=1, source_target_pairs={{0,1},{1,2},{2,3},{4,5},{5,6},{6,7},{8,9},{9,10},{10,11},{12,13},{... | collective-permute-start | bytes 442376 | tf_op jit(solution)/shard_map/ppermute | solution.py:14
  14.4 2.0 slice_reduce_fusion.48
  16.4 1.3 slice_reduce_fusion.46
  17.7 0.0 copy-start.4
  17.7 1.8 slice_reduce_fusion.47
  19.7 0.2 select_maximum_fusion.2
  20.0 0.0 copy-start.3
  20.0 0.0 copy-start.50
  20.0 3.4 fusion.158
  23.6 0.0 copy-start.1
  23.6 0.0 copy-start.53
  23.6 0.2 multiply_reduce_fusion.2
  23.8 0.4 copy-done.46
  24.2 0.6 copy-done.48
  24.8 0.1 add_convert_fusion.1
  24.9 6.9 %all_gather.6 = bf16[12,16,1536]{2,1,0:T(8,128)(2,1)S(1)} all-gather(bf16[3,16,1536]{2,1,0:T(8,128)(2,1)S(1)} %add_convert_fusion.1), channel_id=1, replica_groups=mesh['fsdp'=8,'rows'=4] {'rows'}, dimensions={0}, use_global_device_ids=true | all-gather | bytes 737280 | tf_op jit(solution)/shard_map/all_gather | solution.py:114
  31.8 59.4 %all-gather.2.cloned.1.call-done = bf16[1536,1536]{1,0:T(8,128)(2,1)} async-done(((bf16[192,1536]{1,0:T(8,128)(2,1)}), bf16[1536,1536]{1,0:T(8,128)(2,1)}) %all-gather.2.cloned.1.call-update) | async-done | bytes 4718608 | tf_op jit(solution)/shard_map/all_gather | solution.py:108
  91.2 7.3 %fusion.9 = (f32[1536]{0:T(1024)S(1)}, f32[1536]{0:T(1024)S(1)}, f32[192,1536]{1,0:T(8,128)}, f32[192,1536]{1,0:T(8,128)}) fusion(bf16[1,12,16,1536]{3,2,1,0:T(8,128)(2,1)S(1)} %copy-done.1, f32[1536]{0:T(1024)S(1)} %copy-done.53, bf16[192,1536]{1,0:T(8,128)(2,1)S(1)} %bitcast.21, bf16[1536,1536]{1,0:T(8,128)(2,1)} %all-gather.2.cloned.1.call-done), kind=kOutput, calls=%fused_computation.65 | convolution fusion | flops 926610432 | bytes 8275968 | tf_op jit(solution)/shard_map/dot_general | solution.py:118
  98.6 0.7 multiply_reduce_fusion.3
  99.2 7.3 %all-reduce.2 = (f32[]{:T(128)}, f32[]{:T(128)}) all-reduce(f32[]{:T(128)} %get-tuple-element.115, f32[]{:T(128)} %get-tuple-element.114), channel_id=1, replica_groups=mesh['fsdp'=8,'rows'=4] {'rows'}, use_global_device_ids=true, to_apply=%region_4.5 | all-reduce | flops 2 | bytes 16 | tf_op jit(solution)/shard_map/psum | solution.py:123
  107.9 3.2 fusion.8
  111.1 4.8 %fusion.2 = bf16[12,16,1536]{2,1,0:T(8,128)(2,1)} fusion(bf16[12,16,1536]{2,1,0:T(8,128)(2,1)S(1)} %bitcast.23, bf16[1536,1536]{1,0:T(8,128)(2,1)} %all-gather.2.cloned.1.call-done), kind=kOutput, calls=%fused_computation.54 | convolution fusion | flops 906264576 | bytes 5898240 | tf_op jit(solution)/shard_map/hwf,cf->hwc/dot_general | solution.py:139
  116.0 0.0 reduce-scatter.3.cloned.1.call-update
  116.0 0.0 reduce-scatter.5.cloned.1.call-start
  116.0 3.6 convolution_convert_fusion
  119.6 0.0 reduce-scatter.5.cloned.1.call-update
  119.6 0.0 all-reduce.5.cloned.1.call-start
  119.7 16.9 %reduce-scatter.3.cloned.1.call-done = bf16[3,16,1536]{2,1,0:T(8,128)(2,1)} async-done(((bf16[12,16,1536]{2,1,0:T(8,128)(2,1)}), bf16[3,16,1536]{2,1,0:T(8,128)(2,1)}) %reduce-scatter.3.cloned.1.call-update) | async-done | bytes 147472 | tf_op jit(solution)/shard_map/reduce_scatter | solution.py:138
  136.6 1.1 fusion.147
  137.7 1.9 fusion.145
  139.6 2.8 collective-permute-start.3
  142.3 3.0 collective-permute-start.2
  145.3 0.8 fusion.146
  146.1 0.6 fusion.136
  147.4 0.5 stack.199
  147.9 0.0 copy-start.5
  148.1 0.8 reshape.62
  148.9 0.0 all-reduce.5.cloned.1.call-update
  148.9 0.2 select_maximum_fusion
  149.3 2.8 fusion.153
  152.1 83.8 %reduce-scatter.5.cloned.1.call-done = bf16[192,1536]{1,0:T(8,128)(2,1)} async-done(((bf16[1536,1536]{1,0:T(8,128)(2,1)}), bf16[192,1536]{1,0:T(8,128)(2,1)}) %reduce-scatter.5.cloned.1.call-update) | async-done | bytes 589840 | tf_op jit(solution)/shard_map/reduce_scatter | solution.py:134
  235.9 2.2 convert_element_type.489
  238.1 130.2 %all-reduce.5.cloned.1.call-done = f32[7,7,1536]{2,1,0:T(8,128)} async-done(((f32[7,7,1536]{2,1,0:T(8,128)}), f32[7,7,1536]{2,1,0:T(8,128)}) %all-reduce.5.cloned.1.call-update) | async-done | bytes 301072 | tf_op jit(solution)/shard_map/psum | solution.py:152
  368.3 1.7 copy.15
  (157 shorter events, 0.6 us)
Async XLA Ops:
  7.2 12.6 %copy-start = (bf16[1,3,16,1536]{3,2,1,0:T(8,128)(2,1)S(1)}, bf16[1,3,16,1536]{3,2,1,0:T(8,128)(2,1)}, u32[]{:S(2)}) copy-start(bf16[1,3,16,1536]{3,2,1,0:T(8,128)(2,1)} %param.10) | copy-start | bytes 442372
  7.2 12.8 %copy-start.52 = (f32[1536]{0:T(1024)S(1)}, f32[1536]{0:T(1024)}, u32[]{:S(2)}) copy-start(f32[1536]{0:T(1024)} %param.12) | copy-start | bytes 18436
  7.2 84.0 %all-gather.2.cloned.1.call-start = ((), (), s32[]{:S(2)}) async-start(), calls=%async_computation.2 | async-start | bytes 5308416 | tf_op jit(solution)/shard_map/all_gather | solution.py:108
  7.9 128.7 %reduce-scatter.3.cloned.1.call-start = ((), (), s32[]{:S(2)}) async-start(), calls=%async_computation.3 | async-start | bytes 737280 | tf_op jit(solution)/shard_map/reduce_scatter | solution.py:138
  8.0 11.7 %collective-permute-start.1 = (bf16[3,16,1536]{2,1,0:T(8,128)(2,1)}, bf16[3,16,1536]{2,1,0:T(8,128)(2,1)S(1)}, u32[]{:S(2)}, u32[]{:S(2)}) collective-permute-start(bf16[3,16,1536]{2,1,0:T(8,128)(2,1)} %bitcast.24), channel_id=1, source_target_pairs={{1,0},{2,1},{3,2},{5,4},{6,5},{7,6},{9,8},{10,9},{11,10},{13,12},{... | collective-permute-start | bytes 442376 | tf_op jit(solution)/shard_map/ppermute | solution.py:17
  9.9 9.8 %collective-permute-start = (bf16[3,16,1536]{2,1,0:T(8,128)(2,1)}, bf16[3,16,1536]{2,1,0:T(8,128)(2,1)S(1)}, u32[]{:S(2)}, u32[]{:S(2)}) collective-permute-start(bf16[3,16,1536]{2,1,0:T(8,128)(2,1)} %bitcast.25), channel_id=1, source_target_pairs={{0,1},{1,2},{2,3},{4,5},{5,6},{6,7},{8,9},{9,10},{10,11},{12,13},{... | collective-permute-start | bytes 442376 | tf_op jit(solution)/shard_map/ppermute | solution.py:14
  17.7 5.7 %copy-start.4 = (f32[1536]{0:T(1024)}, f32[1536]{0:T(1024)S(1)}, u32[]{:S(2)}) copy-start(f32[1536]{0:T(1024)S(1)} %get-tuple-element.99) | copy-start | bytes 18436
  17.7 5.7 %copy-start.6 = (f32[1536]{0:T(1024)}, f32[1536]{0:T(1024)S(1)}, u32[]{:S(2)}) copy-start(f32[1536]{0:T(1024)S(1)} %get-tuple-element.100) | copy-start | bytes 18436
  19.5 3.9 %copy-start.8 = (f32[1536]{0:T(1024)}, f32[1536]{0:T(1024)S(1)}, u32[]{:S(2)}) copy-start(f32[1536]{0:T(1024)S(1)} %get-tuple-element.71) | copy-start | bytes 18436
  19.5 3.9 %copy-start.10 = (f32[1536]{0:T(1024)}, f32[1536]{0:T(1024)S(1)}, u32[]{:S(2)}) copy-start(f32[1536]{0:T(1024)S(1)} %get-tuple-element.72) | copy-start | bytes 18436
  19.5 3.9 %copy-start.12 = (f32[1536]{0:T(1024)}, f32[1536]{0:T(1024)S(1)}, u32[]{:S(2)}) copy-start(f32[1536]{0:T(1024)S(1)} %get-tuple-element.73) | copy-start | bytes 18436
  19.5 3.9 %copy-start.14 = (f32[1536]{0:T(1024)}, f32[1536]{0:T(1024)S(1)}, u32[]{:S(2)}) copy-start(f32[1536]{0:T(1024)S(1)} %get-tuple-element.74) | copy-start | bytes 18436
  19.5 3.9 %copy-start.16 = (f32[1536]{0:T(1024)}, f32[1536]{0:T(1024)S(1)}, u32[]{:S(2)}) copy-start(f32[1536]{0:T(1024)S(1)} %get-tuple-element.75) | copy-start | bytes 18436
  19.6 3.9 %copy-start.18 = (f32[1536]{0:T(1024)}, f32[1536]{0:T(1024)S(1)}, u32[]{:S(2)}) copy-start(f32[1536]{0:T(1024)S(1)} %get-tuple-element.76) | copy-start | bytes 18436
  19.6 3.9 %copy-start.20 = (f32[1536]{0:T(1024)}, f32[1536]{0:T(1024)S(1)}, u32[]{:S(2)}) copy-start(f32[1536]{0:T(1024)S(1)} %get-tuple-element.77) | copy-start | bytes 18436
  19.6 3.9 %copy-start.22 = (f32[1536]{0:T(1024)}, f32[1536]{0:T(1024)S(1)}, u32[]{:S(2)}) copy-start(f32[1536]{0:T(1024)S(1)} %get-tuple-element.78) | copy-start | bytes 18436
  19.6 3.9 %copy-start.24 = (f32[1536]{0:T(1024)}, f32[1536]{0:T(1024)S(1)}, u32[]{:S(2)}) copy-start(f32[1536]{0:T(1024)S(1)} %get-tuple-element.79) | copy-start | bytes 18436
  19.6 3.9 %copy-start.26 = (f32[1536]{0:T(1024)}, f32[1536]{0:T(1024)S(1)}, u32[]{:S(2)}) copy-start(f32[1536]{0:T(1024)S(1)} %get-tuple-element.80) | copy-start | bytes 18436
  19.6 3.9 %copy-start.28 = (f32[1536]{0:T(1024)}, f32[1536]{0:T(1024)S(1)}, u32[]{:S(2)}) copy-start(f32[1536]{0:T(1024)S(1)} %get-tuple-element.81) | copy-start | bytes 18436
  19.6 3.9 %copy-start.30 = (f32[1536]{0:T(1024)}, f32[1536]{0:T(1024)S(1)}, u32[]{:S(2)}) copy-start(f32[1536]{0:T(1024)S(1)} %get-tuple-element.82) | copy-start | bytes 18436
  19.6 3.9 %copy-start.32 = (f32[1536]{0:T(1024)}, f32[1536]{0:T(1024)S(1)}, u32[]{:S(2)}) copy-start(f32[1536]{0:T(1024)S(1)} %get-tuple-element.83) | copy-start | bytes 18436
  19.6 3.9 %copy-start.34 = (f32[1536]{0:T(1024)}, f32[1536]{0:T(1024)S(1)}, u32[]{:S(2)}) copy-start(f32[1536]{0:T(1024)S(1)} %get-tuple-element.84) | copy-start | bytes 18436
  19.6 3.9 %copy-start.36 = (f32[1536]{0:T(1024)}, f32[1536]{0:T(1024)S(1)}, u32[]{:S(2)}) copy-start(f32[1536]{0:T(1024)S(1)} %get-tuple-element.85) | copy-start | bytes 18436
  19.7 3.9 %copy-start.38 = (f32[1536]{0:T(1024)}, f32[1536]{0:T(1024)S(1)}, u32[]{:S(2)}) copy-start(f32[1536]{0:T(1024)S(1)} %get-tuple-element.86) | copy-start | bytes 18436
  19.7 3.9 %copy-start.40 = (f32[1536]{0:T(1024)}, f32[1536]{0:T(1024)S(1)}, u32[]{:S(2)}) copy-start(f32[1536]{0:T(1024)S(1)} %get-tuple-element.87) | copy-start | bytes 18436
  19.7 3.9 %copy-start.42 = (f32[1536]{0:T(1024)}, f32[1536]{0:T(1024)S(1)}, u32[]{:S(2)}) copy-start(f32[1536]{0:T(1024)S(1)} %get-tuple-element.88) | copy-start | bytes 18436
  19.7 3.9 %copy-start.44 = (f32[1536]{0:T(1024)}, f32[1536]{0:T(1024)S(1)}, u32[]{:S(2)}) copy-start(f32[1536]{0:T(1024)S(1)} %get-tuple-element.89) | copy-start | bytes 18436
  20.0 4.8 %copy-start.3 = (f32[1536]{0:T(1024)S(1)}, f32[1536]{0:T(1024)}, u32[]{:S(2)}) copy-start(f32[1536]{0:T(1024)} %param.13) | copy-start | bytes 18436
  20.0 4.8 %copy-start.50 = (f32[1536]{0:T(1024)S(1)}, f32[1536]{0:T(1024)}, u32[]{:S(2)}) copy-start(f32[1536]{0:T(1024)} %param.14) | copy-start | bytes 18436
  23.6 67.6 %copy-start.1 = (bf16[1,12,16,1536]{3,2,1,0:T(8,128)(2,1)S(1)}, bf16[1,12,16,1536]{3,2,1,0:T(8,128)(2,1)}, u32[]{:S(2)}) copy-start(bf16[1,12,16,1536]{3,2,1,0:T(8,128)(2,1)} %param.19) | copy-start | bytes 1769476
  23.6 67.6 %copy-start.53 = (f32[1536]{0:T(1024)S(1)}, f32[1536]{0:T(1024)}, u32[]{:S(2)}) copy-start(f32[1536]{0:T(1024)} %param.16) | copy-start | bytes 18436
  91.2 7.4 %copy-start.2 = (f32[1536]{0:T(1024)S(1)}, f32[1536]{0:T(1024)}, u32[]{:S(2)}) copy-start(f32[1536]{0:T(1024)} %param.17) | copy-start | bytes 18436
  91.2 16.7 %copy-start.51 = (f32[1536]{0:T(1024)S(1)}, f32[1536]{0:T(1024)}, u32[]{:S(2)}) copy-start(f32[1536]{0:T(1024)} %param.18) | copy-start | bytes 18436
  116.0 119.9 %reduce-scatter.5.cloned.1.call-start = ((), (), s32[]{:S(2)}) async-start(), calls=%async_computation.4 | async-start | bytes 5308416 | tf_op jit(solution)/shard_map/reduce_scatter | solution.py:134
  119.6 17.0 %copy-start.47 = (f32[3,16]{1,0:T(4,128)S(1)}, f32[3,16]{1,0:T(4,128)}, u32[]{:S(2)}) copy-start(f32[3,16]{1,0:T(4,128)} %copy-done.46) | copy-start | bytes 580
  119.6 17.0 %copy-start.49 = (f32[3,16]{1,0:T(4,128)S(1)}, f32[3,16]{1,0:T(4,128)}, u32[]{:S(2)}) copy-start(f32[3,16]{1,0:T(4,128)} %copy-done.48) | copy-start | bytes 580
  119.6 248.7 %all-reduce.5.cloned.1.call-start = ((), (), s32[]{:S(2)}) async-start(), calls=%async_computation.5 | async-start | bytes 688128 | tf_op jit(solution)/shard_map/psum | solution.py:152
  139.6 9.3 %collective-permute-start.3 = (bf16[3,16,1536]{2,1,0:T(8,128)(2,1)S(1)}, bf16[3,16,1536]{2,1,0:T(8,128)(2,1)S(1)}, u32[]{:S(2)}, u32[]{:S(2)}) collective-permute-start(bf16[3,16,1536]{2,1,0:T(8,128)(2,1)S(1)} %get-tuple-element.118), channel_id=1, source_target_pairs={{1,0},{2,1},{3,2},{5,4},{6,5},{7,6},{9,8},{10,9},{11,10},{13,12},{... | collective-permute-start | bytes 442376 | tf_op jit(solution)/shard_map/ppermute | solution.py:17
  142.3 6.6 %collective-permute-start.2 = (bf16[3,16,1536]{2,1,0:T(8,128)(2,1)S(1)}, bf16[3,16,1536]{2,1,0:T(8,128)(2,1)S(1)}, u32[]{:S(2)}, u32[]{:S(2)}) collective-permute-start(bf16[3,16,1536]{2,1,0:T(8,128)(2,1)S(1)} %get-tuple-element.118), channel_id=1, source_target_pairs={{0,1},{1,2},{2,3},{4,5},{5,6},{6,7},{8,9},{9,10},{10,11},{12,13},{... | collective-permute-start | bytes 442376 | tf_op jit(solution)/shard_map/ppermute | solution.py:14
  147.9 1.3 copy-start.5
  147.9 1.3 copy-start.7
  147.9 1.3 copy-start.9
  147.9 1.3 copy-start.11
  147.9 1.3 copy-start.13
  147.9 1.3 copy-start.15
  147.9 1.3 copy-start.17
  147.9 1.3 copy-start.19
  148.0 1.3 copy-start.21
  (14 other events, 16.2 us)
Sparse Core Ops, SparseCore 0:
  10.2 80.9 all-gather.1
  116.1 20.4 reduce-scatter.2
  140.3 95.5 reduce-scatter.4
  241.7 126.5 all-reduce.4
where the time goes:
time: 377 us
  waiting for transfers between devices  291 us (77%)
  other arithmetic  17.4 us (5%)
  between operations  16.3 us (4%)
  matrix products  15.7 us (4%)
  blocking collectives  14.2 us (4%)
  starting transfers between devices  12.3 us (3%)
  local copies, waits for them, and re-layouts  9.57 us (3%)
    psum x1, waiting for transfers between devices, body(): kernel_total = lax.psum(kernel_local, ('fsdp', 'rows'))  130 us
    reduce_scatter x1, waiting for transfers between devices, body(): lax.psum_scatter(w_term.astype(jnp.bfloat16), 'fsdp', scatter_dimension=0...  83.8 us
    all_gather x1, waiting for transfers between devices, body(): columns = lax.all_gather(up_weight, 'fsdp', axis=0, tiled=True)  59.4 us
    reduce_scatter x1, waiting for transfers between devices, body(): lax.psum_scatter(jnp.einsum('hwf,cf->hwc', dpre_rows, columns, preferred_...  16.9 us
  transfers between devices with their start and end apart: 8, of which 4 were waited for; matrix products, arithmetic and copies ran while one was open for 6% of the time, Pallas kernels for 0%

commit v1 on v0

--- a/solution.py
+++ b/solution.py
@@ -1,9 +1,18 @@
+import functools
 import jax
 import jax.numpy as jnp
 from jax import lax
 from jax.sharding import PartitionSpec as P
 
 FF = 6144
+
+
+def bring_scales_on(piece_in, axis_id):
+    part_now = lax.all_gather(piece_in, axis_name=axis_id)
+    return jnp.sum(part_now, 0)
+
+
+list_units_up = functools.partial(bring_scales_on, axis_id=("fsdp", "rows"))
 
 
 def extended(block, sides, width):
@@ -149,7 +158,7 @@
     grad_pad = extended(activation_gradient, (("rows", 0),), 3)
     dframe = back_conv(grad_pad, kernel).astype(jnp.bfloat16)
     kernel_local = kern_grad(padded, activation_gradient)
-    kernel_total = lax.psum(kernel_local, ("fsdp", "rows"))
+    kernel_total = list_units_up(kernel_local)
     activation = output.reshape(1, height, cols, -1)
     return (activation, dframe.reshape((1,) + dframe.shape), up_grad, kernel_total)
 

time: 377 us -> 342 us (0.907)
  waiting for transfers between devices: 291 us -> 251 us
  other arithmetic: 17.4 us -> 23.5 us
    psum x1 -> x0, waiting for transfers between devices: 130 us -> none  [body(): kernel_total = lax.psum(kernel_local, ('fsdp', 'rows'))]
    all_gather x0 -> x1, waiting for transfers between devices: none -> 90.3 us  [bring_scales_on(): part_now = lax.all_gather(piece_in, axis_name=axis_id)]
    reduce_sum x0 -> x1, other arithmetic: none -> 6.18 us  [bring_scales_on(): return jnp.sum(part_now, 0)]
  transfers between devices with their start and end apart: 8 -> 8, of which waited for: 4 -> 6; matrix products, arithmetic and copies ran while one was open for 6% -> 7% of each run, Pallas kernels for 0% -> 0%
where the time goes in v1:
time: 342 us; the launch traced here: 341 us
  waiting for transfers between devices  251 us (73%)
  other arithmetic  23.5 us (7%)
  between operations  16.2 us (5%)
  matrix products  15.8 us (5%)
  blocking collectives  14.2 us (4%)
  starting transfers between devices  12.3 us (4%)
  local copies, waits for them, and re-layouts  7.76 us (2%)
    all_gather x1, waiting for transfers between devices, bring_scales_on(): part_now = lax.all_gather(piece_in, axis_name=axis_id)  90.3 us
    reduce_scatter x1, waiting for transfers between devices, body(): lax.psum_scatter(w_term.astype(jnp.bfloat16), 'fsdp', scatter_dimension=0...  81.5 us
    all_gather x1, waiting for transfers between devices, body(): columns = lax.all_gather(up_weight, 'fsdp', axis=0, tiled=True)  59.5 us
    reduce_scatter x1, waiting for transfers between devices, body(): lax.psum_scatter(jnp.einsum('hwf,cf->hwc', dpre_rows, columns, preferred_...  16.6 us
    ppermute x2, starting transfers between devices, extended(): lax.ppermute(lax.slice_in_dim(block, block.shape[dim] - width, None, axis...  7.45 us
    dot_general x1, matrix products, body(): pre = jnp.dot(flat, columns, preferred_element_type=jnp.float32) + up_bias  7.34 us
    psum x1, blocking collectives, body(): norm_total = lax.psum(jnp.sum(norms), 'rows')  7.3 us
    all_gather x1, blocking collectives, body(): whole = lax.all_gather(normed_output, 'rows', axis=0, tiled=True)  6.86 us
  transfers between devices with their start and end apart: 8, of which 6 were waited for; matrix products, arithmetic and copies ran while one was open for 7% of the time, Pallas kernels for 0%

profile of v1, /device:TPU:1, one launch (start us, length us, event | category | flops | bytes accessed | tf_op | source)
XLA Modules:
  0.0 340.6 jit_solution(8635793611127891942)
XLA Ops:
  7.2 0.0 all-gather.3.cloned.1.call-start
  7.2 0.7 all-gather.3.cloned.1.call-update
  7.9 0.0 reduce-scatter.3.cloned.1.call-start
  8.0 2.0 collective-permute-start.1
  9.9 4.5 %collective-permute-start = (bf16[3,16,1536]{2,1,0:T(8,128)(2,1)}, bf16[3,16,1536]{2,1,0:T(8,128)(2,1)S(1)}, u32[]{:S(2)}, u32[]{:S(2)}) collective-permute-start(bf16[3,16,1536]{2,1,0:T(8,128)(2,1)} %bitcast.25), channel_id=1, source_target_pairs={{0,1},{1,2},{2,3},{4,5},{5,6},{6,7},{8,9},{9,10},{10,11},{12,13},{... | collective-permute-start | bytes 442376 | tf_op jit(solution)/shard_map/ppermute | solution.py:23
  14.4 1.8 slice_reduce_fusion.48
  16.2 1.4 slice_reduce_fusion.46
  17.6 0.0 copy-start.4
  17.6 1.8 slice_reduce_fusion.47
  19.6 0.2 select_maximum_fusion.2
  19.9 0.0 copy-start.50
  19.9 3.4 %fusion.158 = (f32[3,16]{1,0:T(4,128)S(1)}, f32[3,16,1536]{2,1,0:T(8,128)S(1)}) fusion(f32[1536]{0:T(1024)S(1)} %get-tuple-element.99, bf16[9,22,1536]{2,1,0:T(8,128)(2,1)S(1)} %select_maximum_fusion.2, f32[1536]{0:T(1024)S(1)} %get-tuple-element.100, f32[1536]{0:T(1024)S(1)} %get-tuple-element.53, f32[1536]{0:T(1024)S(1)} %get-tuple-element.54, ...), kind=kLoop, calls=%fused_computation.350 | loop fusion | flops 11206608 | bytes 7237824 | tf_op jit(solution)/shard_map/reduce_sum | solution.py:71
  23.5 0.0 copy-start.1
  23.5 0.0 copy-start.53
  23.5 0.2 multiply_reduce_fusion.2
  23.7 0.4 copy-done.46
  24.1 0.6 copy-done.48
  24.7 0.1 add_convert_fusion.1
  24.8 6.9 %all_gather.9 = bf16[12,16,1536]{2,1,0:T(8,128)(2,1)S(1)} all-gather(bf16[3,16,1536]{2,1,0:T(8,128)(2,1)S(1)} %add_convert_fusion.1), channel_id=1, replica_groups=mesh['fsdp'=8,'rows'=4] {'rows'}, dimensions={0}, use_global_device_ids=true | all-gather | bytes 737280 | tf_op jit(solution)/shard_map/all_gather | solution.py:123
  31.7 59.5 %all-gather.3.cloned.1.call-done = bf16[1536,1536]{1,0:T(8,128)(2,1)} async-done(((bf16[192,1536]{1,0:T(8,128)(2,1)}), bf16[1536,1536]{1,0:T(8,128)(2,1)}) %all-gather.3.cloned.1.call-update) | async-done | bytes 4718608 | tf_op jit(solution)/shard_map/all_gather | solution.py:117
  91.2 7.3 %fusion.9 = (f32[1536]{0:T(1024)S(1)}, f32[1536]{0:T(1024)S(1)}, f32[192,1536]{1,0:T(8,128)}, f32[192,1536]{1,0:T(8,128)}) fusion(bf16[1,12,16,1536]{3,2,1,0:T(8,128)(2,1)S(1)} %copy-done.1, f32[1536]{0:T(1024)S(1)} %copy-done.53, bf16[192,1536]{1,0:T(8,128)(2,1)S(1)} %bitcast.21, bf16[1536,1536]{1,0:T(8,128)(2,1)} %all-gather.3.cloned.1.call-done), kind=kOutput, calls=%fused_computation.65 | convolution fusion | flops 926610432 | bytes 8275968 | tf_op jit(solution)/shard_map/dot_general | solution.py:127
  98.6 0.6 multiply_reduce_fusion.3
  99.2 7.3 %all-reduce.2 = (f32[]{:T(128)}, f32[]{:T(128)}) all-reduce(f32[]{:T(128)} %get-tuple-element.115, f32[]{:T(128)} %get-tuple-element.114), channel_id=1, replica_groups=mesh['fsdp'=8,'rows'=4] {'rows'}, use_global_device_ids=true, to_apply=%region_4.5 | all-reduce | flops 2 | bytes 16 | tf_op jit(solution)/shard_map/psum | solution.py:132
  107.8 3.2 fusion.8
  111.0 4.8 %fusion.2 = bf16[12,16,1536]{2,1,0:T(8,128)(2,1)} fusion(bf16[12,16,1536]{2,1,0:T(8,128)(2,1)S(1)} %bitcast.23, bf16[1536,1536]{1,0:T(8,128)(2,1)} %all-gather.3.cloned.1.call-done), kind=kOutput, calls=%fused_computation.54 | convolution fusion | flops 906264576 | bytes 5898240 | tf_op jit(solution)/shard_map/hwf,cf->hwc/dot_general | solution.py:148
  115.8 0.0 reduce-scatter.3.cloned.1.call-update
  115.9 0.0 reduce-scatter.5.cloned.1.call-start
  115.9 3.6 %convolution_convert_fusion = bf16[1536,1536]{1,0:T(8,128)(2,1)} fusion(bf16[192,1536]{1,0:T(8,128)(2,1)S(1)} %bitcast.22, bf16[192,1536]{1,0:T(8,128)(2,1)S(1)} %get-tuple-element.124), kind=kOutput, calls=%fused_computation | convolution fusion | flops 908328960 | bytes 5898240 | tf_op jit(solution)/shard_map/dot_general | solution.py:140
  119.5 0.0 reduce-scatter.5.cloned.1.call-update
  119.6 0.2 all-gather.5.cloned.1.call-start
  119.8 16.6 %reduce-scatter.3.cloned.1.call-done = bf16[3,16,1536]{2,1,0:T(8,128)(2,1)} async-done(((bf16[12,16,1536]{2,1,0:T(8,128)(2,1)}), bf16[3,16,1536]{2,1,0:T(8,128)(2,1)}) %reduce-scatter.3.cloned.1.call-update) | async-done | bytes 147472 | tf_op jit(solution)/shard_map/reduce_scatter | solution.py:147
  136.4 1.1 fusion.147
  137.6 1.9 fusion.145
  139.4 0.6 fusion.136
  140.0 0.8 fusion.146
  141.4 0.5 stack.199
  142.2 0.8 all_gather_reshape.3
  142.9 0.0 all-gather.5.cloned.1.call-update
  143.0 2.6 collective-permute-start.3
  145.5 3.0 collective-permute-start.2
  148.5 0.9 collective-permute-done.3
  149.4 1.2 collective-permute-done.2
  150.6 0.2 select_maximum_fusion
  151.1 2.8 fusion.153
  153.8 81.5 %reduce-scatter.5.cloned.1.call-done = bf16[192,1536]{1,0:T(8,128)(2,1)} async-done(((bf16[1536,1536]{1,0:T(8,128)(2,1)}), bf16[192,1536]{1,0:T(8,128)(2,1)}) %reduce-scatter.5.cloned.1.call-update) | async-done | bytes 589840 | tf_op jit(solution)/shard_map/reduce_scatter | solution.py:143
  235.4 2.2 convert_element_type.489
  237.6 90.3 %all-gather.5.cloned.1.call-done = f32[32,7,7,1536]{3,2,1,0:T(8,128)} async-done(((f32[1,7,7,1536]{3,2,1,0:T(8,128)}), f32[32,7,7,1536]{3,2,1,0:T(8,128)}) %all-gather.5.cloned.1.call-update) | async-done | bytes 9633808 | tf_op jit(solution)/shard_map/all_gather | solution.py:11
  327.8 6.2 %reduce_sum.579 = f32[7,7,1536]{2,1,0:T(8,128)} reduce(f32[32,7,7,1536]{3,2,1,0:T(8,128)} %all-gather.5.cloned.1.call-done, f32[]{:T(128)} %constant.37.clone.1), dimensions={0}, to_apply=%region_61.62 | reduce | flops 2333184 | bytes 9934852 | tf_op jit(solution)/shard_map/reduce_sum | solution.py:12
  (157 shorter events, 0.6 us)
Async XLA Ops:
  7.2 12.5 %copy-start = (bf16[1,3,16,1536]{3,2,1,0:T(8,128)(2,1)S(1)}, bf16[1,3,16,1536]{3,2,1,0:T(8,128)(2,1)}, u32[]{:S(2)}) copy-start(bf16[1,3,16,1536]{3,2,1,0:T(8,128)(2,1)} %param.10) | copy-start | bytes 442372
  7.2 12.7 %copy-start.52 = (f32[1536]{0:T(1024)S(1)}, f32[1536]{0:T(1024)}, u32[]{:S(2)}) copy-start(f32[1536]{0:T(1024)} %param.12) | copy-start | bytes 18436
  7.2 84.0 %all-gather.3.cloned.1.call-start = ((), (), s32[]{:S(2)}) async-start(), calls=%async_computation.2 | async-start | bytes 5308416 | tf_op jit(solution)/shard_map/all_gather | solution.py:117
  7.9 128.5 %reduce-scatter.3.cloned.1.call-start = ((), (), s32[]{:S(2)}) async-start(), calls=%async_computation.3 | async-start | bytes 737280 | tf_op jit(solution)/shard_map/reduce_scatter | solution.py:147
  8.0 11.6 %collective-permute-start.1 = (bf16[3,16,1536]{2,1,0:T(8,128)(2,1)}, bf16[3,16,1536]{2,1,0:T(8,128)(2,1)S(1)}, u32[]{:S(2)}, u32[]{:S(2)}) collective-permute-start(bf16[3,16,1536]{2,1,0:T(8,128)(2,1)} %bitcast.24), channel_id=1, source_target_pairs={{1,0},{2,1},{3,2},{5,4},{6,5},{7,6},{9,8},{10,9},{11,10},{13,12},{... | collective-permute-start | bytes 442376 | tf_op jit(solution)/shard_map/ppermute | solution.py:26
  9.9 9.7 %collective-permute-start = (bf16[3,16,1536]{2,1,0:T(8,128)(2,1)}, bf16[3,16,1536]{2,1,0:T(8,128)(2,1)S(1)}, u32[]{:S(2)}, u32[]{:S(2)}) collective-permute-start(bf16[3,16,1536]{2,1,0:T(8,128)(2,1)} %bitcast.25), channel_id=1, source_target_pairs={{0,1},{1,2},{2,3},{4,5},{5,6},{6,7},{8,9},{9,10},{10,11},{12,13},{... | collective-permute-start | bytes 442376 | tf_op jit(solution)/shard_map/ppermute | solution.py:23
  17.6 5.8 %copy-start.4 = (f32[1536]{0:T(1024)}, f32[1536]{0:T(1024)S(1)}, u32[]{:S(2)}) copy-start(f32[1536]{0:T(1024)S(1)} %get-tuple-element.99) | copy-start | bytes 18436
  17.6 5.7 %copy-start.6 = (f32[1536]{0:T(1024)}, f32[1536]{0:T(1024)S(1)}, u32[]{:S(2)}) copy-start(f32[1536]{0:T(1024)S(1)} %get-tuple-element.100) | copy-start | bytes 18436
  19.4 3.9 %copy-start.8 = (f32[1536]{0:T(1024)}, f32[1536]{0:T(1024)S(1)}, u32[]{:S(2)}) copy-start(f32[1536]{0:T(1024)S(1)} %get-tuple-element.71) | copy-start | bytes 18436
  19.4 3.9 %copy-start.10 = (f32[1536]{0:T(1024)}, f32[1536]{0:T(1024)S(1)}, u32[]{:S(2)}) copy-start(f32[1536]{0:T(1024)S(1)} %get-tuple-element.72) | copy-start | bytes 18436
  19.4 3.9 %copy-start.12 = (f32[1536]{0:T(1024)}, f32[1536]{0:T(1024)S(1)}, u32[]{:S(2)}) copy-start(f32[1536]{0:T(1024)S(1)} %get-tuple-element.73) | copy-start | bytes 18436
  19.4 3.9 %copy-start.14 = (f32[1536]{0:T(1024)}, f32[1536]{0:T(1024)S(1)}, u32[]{:S(2)}) copy-start(f32[1536]{0:T(1024)S(1)} %get-tuple-element.74) | copy-start | bytes 18436
  19.4 3.9 %copy-start.16 = (f32[1536]{0:T(1024)}, f32[1536]{0:T(1024)S(1)}, u32[]{:S(2)}) copy-start(f32[1536]{0:T(1024)S(1)} %get-tuple-element.75) | copy-start | bytes 18436
  19.5 3.9 %copy-start.18 = (f32[1536]{0:T(1024)}, f32[1536]{0:T(1024)S(1)}, u32[]{:S(2)}) copy-start(f32[1536]{0:T(1024)S(1)} %get-tuple-element.76) | copy-start | bytes 18436
  19.5 3.9 %copy-start.20 = (f32[1536]{0:T(1024)}, f32[1536]{0:T(1024)S(1)}, u32[]{:S(2)}) copy-start(f32[1536]{0:T(1024)S(1)} %get-tuple-element.77) | copy-start | bytes 18436
  19.9 4.8 %copy-start.3 = (f32[1536]{0:T(1024)S(1)}, f32[1536]{0:T(1024)}, u32[]{:S(2)}) copy-start(f32[1536]{0:T(1024)} %param.13) | copy-start | bytes 18436
  19.9 4.8 %copy-start.50 = (f32[1536]{0:T(1024)S(1)}, f32[1536]{0:T(1024)}, u32[]{:S(2)}) copy-start(f32[1536]{0:T(1024)} %param.14) | copy-start | bytes 18436
  23.5 67.7 %copy-start.1 = (bf16[1,12,16,1536]{3,2,1,0:T(8,128)(2,1)S(1)}, bf16[1,12,16,1536]{3,2,1,0:T(8,128)(2,1)}, u32[]{:S(2)}) copy-start(bf16[1,12,16,1536]{3,2,1,0:T(8,128)(2,1)} %param.19) | copy-start | bytes 1769476
  23.5 67.7 %copy-start.53 = (f32[1536]{0:T(1024)S(1)}, f32[1536]{0:T(1024)}, u32[]{:S(2)}) copy-start(f32[1536]{0:T(1024)} %param.16) | copy-start | bytes 18436
  91.2 7.4 %copy-start.2 = (f32[1536]{0:T(1024)S(1)}, f32[1536]{0:T(1024)}, u32[]{:S(2)}) copy-start(f32[1536]{0:T(1024)} %param.17) | copy-start | bytes 18436
  91.2 16.5 %copy-start.51 = (f32[1536]{0:T(1024)S(1)}, f32[1536]{0:T(1024)}, u32[]{:S(2)}) copy-start(f32[1536]{0:T(1024)} %param.18) | copy-start | bytes 18436
  115.9 119.5 %reduce-scatter.5.cloned.1.call-start = ((), (), s32[]{:S(2)}) async-start(), calls=%async_computation.4 | async-start | bytes 5308416 | tf_op jit(solution)/shard_map/reduce_scatter | solution.py:143
  119.5 16.9 %copy-start.47 = (f32[3,16]{1,0:T(4,128)S(1)}, f32[3,16]{1,0:T(4,128)}, u32[]{:S(2)}) copy-start(f32[3,16]{1,0:T(4,128)} %copy-done.46) | copy-start | bytes 580
  119.5 16.9 %copy-start.49 = (f32[3,16]{1,0:T(4,128)S(1)}, f32[3,16]{1,0:T(4,128)}, u32[]{:S(2)}) copy-start(f32[3,16]{1,0:T(4,128)} %copy-done.48) | copy-start | bytes 580
  119.6 208.3 %all-gather.5.cloned.1.call-start = ((), (), s32[]{:S(2)}) async-start(), calls=%async_computation.5 | async-start | bytes 11354112 | tf_op jit(solution)/shard_map/all_gather | solution.py:11
  142.0 8.9 %copy-start.5 = (f32[1536]{0:T(1024)S(1)}, f32[1536]{0:T(1024)}, u32[]{:S(2)}) copy-start(f32[1536]{0:T(1024)} %copy-done.4) | copy-start | bytes 18436
  142.0 8.9 %copy-start.7 = (f32[1536]{0:T(1024)S(1)}, f32[1536]{0:T(1024)}, u32[]{:S(2)}) copy-start(f32[1536]{0:T(1024)} %copy-done.6) | copy-start | bytes 18436
  142.0 8.9 %copy-start.9 = (f32[1536]{0:T(1024)S(1)}, f32[1536]{0:T(1024)}, u32[]{:S(2)}) copy-start(f32[1536]{0:T(1024)} %copy-done.8) | copy-start | bytes 18436
  142.0 8.9 %copy-start.11 = (f32[1536]{0:T(1024)S(1)}, f32[1536]{0:T(1024)}, u32[]{:S(2)}) copy-start(f32[1536]{0:T(1024)} %copy-done.10) | copy-start | bytes 18436
  142.0 8.9 %copy-start.13 = (f32[1536]{0:T(1024)S(1)}, f32[1536]{0:T(1024)}, u32[]{:S(2)}) copy-start(f32[1536]{0:T(1024)} %copy-done.12) | copy-start | bytes 18436
  142.0 8.9 %copy-start.15 = (f32[1536]{0:T(1024)S(1)}, f32[1536]{0:T(1024)}, u32[]{:S(2)}) copy-start(f32[1536]{0:T(1024)} %copy-done.14) | copy-start | bytes 18436
  142.0 8.9 %copy-start.17 = (f32[1536]{0:T(1024)S(1)}, f32[1536]{0:T(1024)}, u32[]{:S(2)}) copy-start(f32[1536]{0:T(1024)} %copy-done.16) | copy-start | bytes 18436
  142.0 8.9 %copy-start.19 = (f32[1536]{0:T(1024)S(1)}, f32[1536]{0:T(1024)}, u32[]{:S(2)}) copy-start(f32[1536]{0:T(1024)} %copy-done.18) | copy-start | bytes 18436
  142.0 8.9 %copy-start.21 = (f32[1536]{0:T(1024)S(1)}, f32[1536]{0:T(1024)}, u32[]{:S(2)}) copy-start(f32[1536]{0:T(1024)} %copy-done.20) | copy-start | bytes 18436
  142.0 8.9 %copy-start.23 = (f32[1536]{0:T(1024)S(1)}, f32[1536]{0:T(1024)}, u32[]{:S(2)}) copy-start(f32[1536]{0:T(1024)} %copy-done.22) | copy-start | bytes 18436
  142.1 8.9 %copy-start.25 = (f32[1536]{0:T(1024)S(1)}, f32[1536]{0:T(1024)}, u32[]{:S(2)}) copy-start(f32[1536]{0:T(1024)} %copy-done.24) | copy-start | bytes 18436
  142.1 8.9 %copy-start.27 = (f32[1536]{0:T(1024)S(1)}, f32[1536]{0:T(1024)}, u32[]{:S(2)}) copy-start(f32[1536]{0:T(1024)} %copy-done.26) | copy-start | bytes 18436
  142.1 8.9 %copy-start.29 = (f32[1536]{0:T(1024)S(1)}, f32[1536]{0:T(1024)}, u32[]{:S(2)}) copy-start(f32[1536]{0:T(1024)} %copy-done.28) | copy-start | bytes 18436
  142.1 8.9 %copy-start.31 = (f32[1536]{0:T(1024)S(1)}, f32[1536]{0:T(1024)}, u32[]{:S(2)}) copy-start(f32[1536]{0:T(1024)} %copy-done.30) | copy-start | bytes 18436
  142.1 8.9 %copy-start.33 = (f32[1536]{0:T(1024)S(1)}, f32[1536]{0:T(1024)}, u32[]{:S(2)}) copy-start(f32[1536]{0:T(1024)} %copy-done.32) | copy-start | bytes 18436
  142.1 8.9 %copy-start.35 = (f32[1536]{0:T(1024)S(1)}, f32[1536]{0:T(1024)}, u32[]{:S(2)}) copy-start(f32[1536]{0:T(1024)} %copy-done.34) | copy-start | bytes 18436
  142.1 8.9 %copy-start.37 = (f32[1536]{0:T(1024)S(1)}, f32[1536]{0:T(1024)}, u32[]{:S(2)}) copy-start(f32[1536]{0:T(1024)} %copy-done.36) | copy-start | bytes 18436
  142.1 8.9 %copy-start.39 = (f32[1536]{0:T(1024)S(1)}, f32[1536]{0:T(1024)}, u32[]{:S(2)}) copy-start(f32[1536]{0:T(1024)} %copy-done.38) | copy-start | bytes 18436
  142.1 8.9 %copy-start.41 = (f32[1536]{0:T(1024)S(1)}, f32[1536]{0:T(1024)}, u32[]{:S(2)}) copy-start(f32[1536]{0:T(1024)} %copy-done.40) | copy-start | bytes 18436
  142.1 8.9 %copy-start.43 = (f32[1536]{0:T(1024)S(1)}, f32[1536]{0:T(1024)}, u32[]{:S(2)}) copy-start(f32[1536]{0:T(1024)} %copy-done.42) | copy-start | bytes 18436
  142.2 8.9 %copy-start.45 = (f32[1536]{0:T(1024)S(1)}, f32[1536]{0:T(1024)}, u32[]{:S(2)}) copy-start(f32[1536]{0:T(1024)} %copy-done.44) | copy-start | bytes 18436
  143.0 6.5 %collective-permute-start.3 = (bf16[3,16,1536]{2,1,0:T(8,128)(2,1)S(1)}, bf16[3,16,1536]{2,1,0:T(8,128)(2,1)S(1)}, u32[]{:S(2)}, u32[]{:S(2)}) collective-permute-start(bf16[3,16,1536]{2,1,0:T(8,128)(2,1)S(1)} %get-tuple-element.118), channel_id=1, source_target_pairs={{1,0},{2,1},{3,2},{5,4},{6,5},{7,6},{9,8},{10,9},{11,10},{13,12},{... | collective-permute-start | bytes 442376 | tf_op jit(solution)/shard_map/ppermute | solution.py:26
  145.5 5.1 %collective-permute-start.2 = (bf16[3,16,1536]{2,1,0:T(8,128)(2,1)S(1)}, bf16[3,16,1536]{2,1,0:T(8,128)(2,1)S(1)}, u32[]{:S(2)}, u32[]{:S(2)}) collective-permute-start(bf16[3,16,1536]{2,1,0:T(8,128)(2,1)S(1)} %get-tuple-element.118), channel_id=1, source_target_pairs={{0,1},{1,2},{2,3},{4,5},{5,6},{6,7},{8,9},{9,10},{10,11},{12,13},{... | collective-permute-start | bytes 442376 | tf_op jit(solution)/shard_map/ppermute | solution.py:23
  (14 other events, 48.0 us)
Sparse Core Ops, SparseCore 0:
  10.2 80.9 all-gather.2
  116.0 20.4 reduce-scatter.2
  140.1 95.2 reduce-scatter.4
  238.7 89.1 all-gather.4
